TPU v7x, 32 devices: a whole 2x2x4 slice. The times are simulated.
32 devices in a mesh: req: 4 (over y, x), exp: 4 (over z), ffn: 2 (over core).
Axes of the slice: x: 2, y: 2, z: 4, core: 2. Of those that a mesh axis runs over, the one named last changes fastest.
Arguments:
- residual: bfloat16 [2048, 2048], P(('req', 'exp')), may hold values from -5 to 5
- queries: bfloat16 [2048, 4608], P(('req', 'exp'), 'ffn'), may hold values from -30 to 30
- new_latent: bfloat16 [2048, 576], P(('req', 'exp')), may hold values from -6 to 6
- cache_pool: bfloat16 [512, 9216], P(('req', 'exp')), may hold values from -5 to 5
- page_table: int32 [8, 64], replicated, may hold values from 0 to 511, as said below
- cached_len: int32 [8], replicated, may hold values from 0 to 1024
- tenant_start: int32 [8], replicated, may hold values from 0 to 512, as said below
- routes: int32 [2048, 6], P(('req', 'exp')), may hold values from 0 to 31, all different within a row; in each aligned block of 64 rows (0 to 63, 64 to 127, ...) at most 16 rows name the same one
- value_up: bfloat16 [512, 1024], P(None, 'ffn'), may hold values from -0.25 to 0.25
- out_proj: bfloat16 [1024, 2048], P('ffn'), may hold values from -0.1875 to 0.1875
- norm_gain: bfloat16 [2048], replicated, may hold values from 0.099609375 to 1.8984375
- router: bfloat16 [2048, 32], replicated, may hold values from -0.125 to 0.125
- gate_weight: bfloat16 [32, 2048, 1408], P('exp', None, 'ffn'), may hold values from -0.125 to 0.125
- up_weight: bfloat16 [32, 2048, 1408], P('exp', None, 'ffn'), may hold values from -0.125 to 0.125
- down_weight: bfloat16 [32, 1408, 2048], P('exp', 'ffn'), may hold values from -0.15625 to 0.15625
Outputs:
- hidden_out: bfloat16 [2048, 2048], P(('req', 'exp'), 'ffn')
- moe_out: bfloat16 [2048, 2048], P(('req', 'exp'), 'ffn')
Inputs may be any that keep to these rules, and one draw needn't show every extreme that they name: `page_table`: row i lists, in order, the pool pages of request i's cache; the 2 requests of group g = i // 2 use pool pages g * 2 * 64 to (g + 1) * 2 * 64 - 1, each exactly once. tenant_start[i] is at most half of cached_len[i]. `routes`: A row names 6 different experts; in each aligned block of 64 rows at most 16 rows name the same expert.
All inputs are finite; a program needn't handle non-finite values.
Results may differ from a plain program's by a relative error of at most 0.025.
Values may be sent and summed in bfloat16 or wider, within the bound.
No kernel may reach another device: no remote copies, remote signals or barrier semaphores. Data moves between devices by JAX's collectives and lax.ppermute only.
A program may use at most 128 MiB of HBM per device.

v0:
```python
import jax
import jax.numpy as jnp
from jax import lax
from jax.sharding import PartitionSpec as P

LATENT = 512
ROPE_DIM = 64
HEAD_DIM = 128
QKD = 576
EXPERTS = 32
TOP = 6
CAPACITY = 16
REQ_GRP = 2
CMAX = 1024
BLOCK_ROWS = 64
EPSILON = 1e-06
NEG_FILL = -1e30


def slot_numbers(route_block):
    expert_ids = lax.broadcasted_iota(jnp.int32, (1, EXPERTS), 1)
    onehot = (route_block[:, None] == expert_ids).astype(jnp.int32)
    before = jnp.cumsum(onehot, axis=0) - onehot
    return jnp.sum(before * onehot, axis=1)


def local(
    residual,
    queries,
    new_latent,
    cache_pool,
    page_table,
    cached_len,
    tenant_start,
    routes,
    value_up,
    out_proj,
    norm_gain,
    router,
    gate_weight,
    up_weight,
    down_weight,
):
    exp_size = lax.axis_size("exp")
    ffn_size = lax.axis_size("ffn")
    req_index = lax.axis_index("req")
    exp_index = lax.axis_index("exp")
    ffn_index = lax.axis_index("ffn")
    token_rows = residual.shape[0]
    feature_count = residual.shape[1]
    fresh_len = token_rows * exp_size // REQ_GRP
    first_token = (req_index * exp_size + exp_index) * token_rows
    request = first_token // fresh_len
    offset = first_token - request * fresh_len
    pool_all, latent_all = (
        lax.all_gather(cache_pool, "exp", axis=0, tiled=True),
        lax.all_gather(new_latent, "exp", axis=0, tiled=True),
    )
    pool_base = req_index * pool_all.shape[0]
    page_rows = page_table[request] - pool_base
    cached_keys = jnp.take(pool_all, page_rows, axis=0).reshape(CMAX, QKD)
    local_request = request - req_index * REQ_GRP
    fresh_keys = lax.dynamic_slice_in_dim(latent_all, local_request * fresh_len, fresh_len, 0)
    all_keys = jnp.concatenate([cached_keys, fresh_keys], axis=0)
    heads_here = queries.shape[1] // QKD
    query_heads = queries.reshape(token_rows, heads_here, QKD)
    scale_factor = (HEAD_DIM + ROPE_DIM) ** (-0.5)
    scores = (
        jnp.einsum("thd,kd->thk", query_heads, all_keys, preferred_element_type=jnp.float32)
        * scale_factor
    )
    key_pos = lax.broadcasted_iota(jnp.int32, (1, CMAX + fresh_len), 1)
    tok_pos = offset + lax.broadcasted_iota(jnp.int32, (token_rows, 1), 0)
    cached_ok = (key_pos >= tenant_start[request]) & (key_pos < cached_len[request])
    fresh_ok = (key_pos >= CMAX) & (key_pos - CMAX <= tok_pos)
    visible = cached_ok | fresh_ok
    scores = jnp.where(visible[:, None, :], scores, NEG_FILL)
    top_score = jnp.max(scores, axis=2, keepdims=True)
    weights = jnp.exp(scores - top_score)
    attn_probs = (weights / jnp.sum(weights, axis=2, keepdims=True)).astype(jnp.bfloat16)
    latent_out = jnp.einsum(
        "thk,kl->thl", attn_probs, all_keys[:, :LATENT], preferred_element_type=jnp.float32
    ).astype(jnp.bfloat16)
    value_heads = value_up.reshape(LATENT, heads_here, HEAD_DIM)
    head_out = jnp.einsum(
        "thl,lhd->thd", latent_out, value_heads, preferred_element_type=jnp.float32
    )
    head_out = head_out.astype(jnp.bfloat16).reshape(token_rows, heads_here * HEAD_DIM)
    partial_value = jnp.dot(head_out, out_proj, preferred_element_type=jnp.float32)
    column_count = feature_count // ffn_size
    attn_cols = lax.psum_scatter(
        partial_value.astype(jnp.bfloat16), "ffn", scatter_dimension=1, tiled=True
    ).astype(jnp.float32)
    residual_cols = lax.dynamic_slice_in_dim(residual, ffn_index * column_count, column_count, 1)
    hidden_out = (residual_cols.astype(jnp.float32) + attn_cols).astype(jnp.bfloat16)
    hidden_wide = hidden_out.astype(jnp.float32)
    square_sum = lax.psum(jnp.sum(hidden_wide * hidden_wide, axis=1, keepdims=True), "ffn")
    mean_square = square_sum / feature_count
    gain_cols = lax.dynamic_slice_in_dim(norm_gain, ffn_index * column_count, column_count, 0)
    normed_cols = (
        hidden_wide * lax.rsqrt(mean_square + EPSILON) * gain_cols.astype(jnp.float32)
    ).astype(jnp.bfloat16)
    normed_grid = lax.all_gather(normed_cols, ("exp", "ffn"), axis=0, tiled=False)
    normed_grid = normed_grid.reshape(exp_size, ffn_size, token_rows, column_count)
    group_rows = exp_size * token_rows
    routes_all = lax.all_gather(routes, "exp", axis=0, tiled=True)
    logits = jnp.einsum(
        "efrc,fck->erk",
        normed_grid,
        router.reshape(ffn_size, column_count, EXPERTS),
        preferred_element_type=jnp.float32,
    ).reshape(group_rows, EXPERTS)
    chosen = jnp.take_along_axis(logits, routes_all, axis=1)
    raised = jnp.exp(chosen)
    gate_weights = raised / jnp.sum(raised, axis=1, keepdims=True)
    blocks = group_rows // BLOCK_ROWS
    slot_within = jax.vmap(slot_numbers)(routes_all.reshape(blocks, BLOCK_ROWS * TOP))
    block_base = lax.broadcasted_iota(jnp.int32, (blocks, 1), 0) * CAPACITY
    slot_index = (slot_within + block_base).reshape(group_rows * TOP)
    slot_count = blocks * CAPACITY
    local_count = gate_weight.shape[0]
    total_slots = local_count * slot_count
    local_expert = routes_all.reshape(group_rows * TOP) - exp_index * local_count
    is_local = (local_expert >= 0) & (local_expert < local_count)
    local_target = jnp.where(is_local, local_expert * slot_count + slot_index, total_slots)
    token_ids = lax.broadcasted_iota(jnp.int32, (group_rows, TOP), 0).reshape(group_rows * TOP)
    slot_token = jnp.zeros((total_slots,), jnp.int32).at[local_target].set(token_ids, mode="drop")
    slot_weight = (
        jnp.zeros((total_slots,), jnp.float32)
        .at[local_target]
        .set(gate_weights.reshape(group_rows * TOP), mode="drop")
    )
    grouped = normed_grid[slot_token // token_rows, :, slot_token % token_rows, :]
    grouped = grouped.reshape(local_count, slot_count, feature_count)
    gate_part = jnp.einsum("jmd,jdf->jmf", grouped, gate_weight, preferred_element_type=jnp.float32)
    up_part = jnp.einsum("jmd,jdf->jmf", grouped, up_weight, preferred_element_type=jnp.float32)
    active = (jax.nn.silu(gate_part) * up_part).astype(jnp.bfloat16)
    outputs = jnp.einsum("jmf,jfd->jmd", active, down_weight, preferred_element_type=jnp.float32)
    weighted = (outputs.reshape(total_slots, feature_count) * slot_weight[:, None]).astype(
        jnp.bfloat16
    )
    row_ids = lax.broadcasted_iota(jnp.int32, (group_rows, 1), 0)
    onehot = (slot_token[None, :] == row_ids).astype(jnp.bfloat16)
    mixture = jnp.einsum(
        "ers,sfc->efrc",
        onehot.reshape(exp_size, token_rows, total_slots),
        weighted.reshape(total_slots, ffn_size, column_count),
        preferred_element_type=jnp.float32,
    ).astype(jnp.bfloat16)
    mixture = mixture.reshape(exp_size * ffn_size * token_rows, column_count)
    moe_out = lax.psum_scatter(mixture, ("exp", "ffn"), scatter_dimension=0, tiled=True)
    return (hidden_out, moe_out)


def solution(mesh):
    in_specs = (
        P(("req", "exp"), None),
        P(("req", "exp"), "ffn"),
        P(("req", "exp"), None),
        P(("req", "exp"), None),
        P(),
        P(),
        P(),
        P(("req", "exp"), None),
        P(None, "ffn"),
        P("ffn", None),
        P(),
        P(),
        P("exp", None, "ffn"),
        P("exp", None, "ffn"),
        P("exp", "ffn", None),
    )
    out_specs = (P(("req", "exp"), "ffn"), P(("req", "exp"), "ffn"))
    return jax.shard_map(local, mesh=mesh, in_specs=in_specs, out_specs=out_specs, check_vma=False)
```

profile of v0, /device:TPU:0, one launch (start us, length us, event | category | flops | bytes accessed | tf_op | source)
XLA Modules:
  0.0 305.1 jit_solution(3223588927788097875)
XLA Ops:
  8.0 2.0 copy.36
  10.9 2.1 copy.24
  14.9 1.3 iota_compare_fusion.2
  16.3 31.2 %all_gather.16 = bf16[512,576]{0,1:T(8,128)(2,1)S(1)} all-gather(bf16[128,576]{0,1:T(8,128)(2,1)S(1)} %copy-done.4), channel_id=1, replica_groups=mesh['req'=4,'exp'=4,'ffn'=2] {'exp'}, dimensions={0}, use_global_device_ids=true | all-gather | bytes 737280 | tf_op jit(solution)/shard_map/all_gather | solution.py:57
  48.2 1.6 and_or_fusion
  49.9 21.1 %all-gather.4.cloned.1.call-done = bf16[128,9216]{1,0:T(8,128)(2,1)} async-done(((bf16[32,9216]{1,0:T(8,128)(2,1)}), bf16[128,9216]{1,0:T(8,128)(2,1)}) %all-gather.4.cloned.1.call-update) | async-done | bytes 2359312 | tf_op jit(solution)/shard_map/all_gather | solution.py:56
  70.9 5.3 %gather_fusion = bf16[64,9216]{1,0:T(8,128)(2,1)} fusion(bf16[128,9216]{1,0:T(8,128)(2,1)} %all-gather.4.cloned.1.call-done, s32[1024]{0:T(1024)S(1)} %pad_clamp_fusion), kind=kCustom, calls=%fused_computation | custom fusion | bytes 2359552 | tf_op jit(solution)/shard_map/jit(_take)/gather | solution.py:61
  76.3 2.2 gather.14
  78.5 1.5 copy.23
  80.0 1.4 broadcast_select_fusion
  81.4 3.0 fusion.72
  84.4 3.9 %fusion.5 = f32[128,4,1280]{0,2,1:T(8,128)} fusion(bf16[128,4,576]{0,2,1:T(8,128)(2,1)} %bitcast.110, bf16[256,576]{0,1:T(8,128)(2,1)} %constant_dynamic-slice_fusion, bf16[1024,576]{0,1:T(8,128)(2,1)S(1)} %broadcast_select_fusion, pred[128,1280]{0,1:T(8,128)(4,1)S(1)} %copy-done.3), kind=kOutput, calls=%fused_computation.12 | convolution fusion | flops 759234560 | bytes 4849664 | tf_op jit(solution)/shard_map/thd,kd->thk/dot_general | solution.py:69
  88.3 3.9 %fusion.27 = bf16[4,128,128]{1,2,0:T(8,128)(2,1)S(1)} fusion(bf16[512,4,128]{0,2,1:T(8,128)(2,1)} %bitcast.111, bf16[1024,576]{0,1:T(8,128)(2,1)S(1)} %broadcast_select_fusion, bf16[256,576]{0,1:T(8,128)(2,1)} %constant_dynamic-slice_fusion, f32[128,4]{0,1:T(4,128)S(1)} %fusion.72, f32[128,4,1280]{0,2,1:T(8,128)} %fusion.5), kind=kOutput, calls=%fused_computation.32 | convolution fusion | flops 743114496 | bytes 7374848 | tf_op jit(solution)/shard_map/thl,lhd->thd/dot_general | solution.py:85
  92.2 1.3 convolution_convert_fusion
  93.6 7.0 %reduce-scatter.3.cloned.1.call-done = bf16[128,1024]{1,0:T(8,128)(2,1)} async-done(((bf16[128,2048]{1,0:T(8,128)(2,1)}), bf16[128,1024]{1,0:T(8,128)(2,1)}) %reduce-scatter.3.cloned.1.call-update) | async-done | bytes 262160 | tf_op jit(solution)/shard_map/reduce_scatter | solution.py:91
  100.6 1.1 fusion.32
  101.8 2.5 psum.7
  105.3 15.2 %all_gather.19 = s32[512,6]{1,0:T(8,128)S(1)} all-gather(s32[128,6]{1,0:T(8,128)S(1)} %copy.26), channel_id=1, replica_groups=mesh['req'=4,'exp'=4,'ffn'=2] {'exp'}, dimensions={0}, use_global_device_ids=true | all-gather | bytes 15360 | tf_op jit(solution)/shard_map/all_gather | solution.py:106
  121.4 6.9 %reduce-window.6 = s32[8,32,3,128]{3,1,2,0:T(8,128)S(1)} reduce-window(s32[8,32,3,128]{3,1,2,0:T(8,128)S(1)} %fusion.38, s32[]{:T(128)} %constant.65.clone.1), window={size=1x1x1x128 pad=0_0x0_0x0_0x127_0}, to_apply=%region_5.6 | reduce-window | flops 12484608 | bytes 786436 | tf_op jit(solution)/shard_map/reduce-window
  129.7 11.8 %scatter_custom_fusion = s32[1024]{0:T(1024)S(1)} fusion(s32[3072]{0:T(1024)S(1)} %bitcast.115, s32[3072]{0:T(1024)S(1)} %reshape.307, s32[]{:T(128)} %constant.65.clone.1), kind=kCustom, calls=%fused_computation.89 | custom fusion | bytes 4100 | tf_op jit(solution)/shard_map/scatter | solution.py:127
  141.5 1.8 copy.31
  144.0 24.9 %gather_fusion.2 = f32[3072]{0:T(1024)S(1)} fusion(f32[512,32]{0,1:T(8,128)S(1)} %convolution_bitcast_fusion, s32[3072]{0:T(1024)S(1)} %reshape.297), kind=kCustom, calls=%fused_computation.2 | custom fusion | bytes 49152 | tf_op jit(solution)/shard_map/jit(take_along_axis)/gather | solution.py:113
  169.6 5.1 %copy.30 = bf16[4,2,128,1024]{3,1,2,0:T(2,128)(2,1)} copy(bf16[4,2,128,1024]{3,2,1,0:T(8,128)(2,1)} %bitcast.105) | data formatting | bytes 4194304 | tf_op jit(solution)/shard_map/reshape | solution.py:104
  174.7 18.4 %gather_fusion.1 = bf16[1024,2,1024]{2,1,0:T(2,128)(2,1)} fusion(bf16[4,2,128,1024]{3,1,2,0:T(2,128)(2,1)} %copy.30, s32[1024]{0:T(1024)S(1)} %fusion.49), kind=kCustom, calls=%fused_computation.1 | custom fusion | bytes 8396800 | tf_op jit(solution)/shard_map/gather | solution.py:133
  193.2 7.8 %reshape.279 = bf16[8,128,2048]{2,1,0:T(8,128)(2,1)} reshape(bf16[1024,2,1024]{2,1,0:T(2,128)(2,1)} %gather_fusion.1) | data formatting | bytes 8388608 | tf_op jit(solution)/shard_map/reshape | solution.py:134
  201.0 12.0 %scatter_custom_fusion.1 = f32[1024]{0:T(1024)S(1)} fusion(s32[3072]{0:T(1024)S(1)} %bitcast.116, f32[3072]{0:T(1024)S(1)} %reshape.315, f32[]{:T(128)} %constant.118.clone.1), kind=kCustom, calls=%fused_computation.92 | custom fusion | bytes 4100 | tf_op jit(solution)/shard_map/scatter | solution.py:131
  213.0 13.1 %fusion.75 = f32[8,128,704]{1,2,0:T(8,128)} fusion(bf16[8,128,2048]{2,1,0:T(8,128)(2,1)} %reshape.279, bf16[8,2048,704]{1,2,0:T(8,128)(2,1)} %param.27), kind=kOutput, calls=%fused_computation.111 | convolution fusion | flops 2952790016 | bytes 30146560 | tf_op jit(solution)/shard_map/jmd,jdf->jmf/dot_general | solution.py:135
  226.1 20.7 %multiply_convert_fusion = bf16[8,128,2048]{2,1,0:T(8,128)(2,1)} fusion(f32[8,128]{1,0:T(8,128)S(1)} %bitcast.117, bf16[8,704,2048]{2,1,0:T(8,128)(2,1)} %param.29, f32[8,128,704]{1,2,0:T(8,128)} %fusion.75, bf16[8,128,2048]{2,1,0:T(8,128)(2,1)} %reshape.279, bf16[8,2048,704]{1,2,0:T(8,128)(2,1)} %param.28), kind=kOutput, calls=%fused_computation.6 | convolution fusion | flops 5914099712 | bytes 57413632 | tf_op jit(solution)/shard_map/jmf,jfd->jmd/dot_general | solution.py:138
  246.8 7.8 %convert_element_type.72 = bf16[1024,2,1024]{2,1,0:T(2,128)(2,1)} reshape(bf16[8,128,2048]{2,1,0:T(8,128)(2,1)} %multiply_convert_fusion) | data formatting | bytes 8388608 | tf_op jit(solution)/shard_map/convert_element_type | solution.py:139
  254.6 4.8 %convert_bitcast_fusion = bf16[4,2,128,1024]{3,2,0,1:T(8,128)(2,1)S(1)} fusion(bf16[1024,2,1024,1]{2,1,0,3:T(2,128)(2,1)} %bitcast.108, s32[4,128]{1,0:T(4,128)S(1)} %multiply_add_fusion, s32[1024]{0:T(1024)S(1)} %scatter_custom_fusion), kind=kOutput, calls=%fused_computation.17 | convolution fusion | flops 2149056512 | bytes 6297600 | tf_op jit(solution)/shard_map/ers,sfc->efrc/dot_general | solution.py:144
  259.3 1.6 copy.34
  261.0 37.6 %reduce-scatter.5.cloned.1.call-done = bf16[128,1024]{1,0:T(8,128)(2,1)} async-done(((bf16[1024,1024]{1,0:T(8,128)(2,1)}), bf16[128,1024]{1,0:T(8,128)(2,1)}) %reduce-scatter.5.cloned.1.call-update) | async-done | bytes 262160 | tf_op jit(solution)/shard_map/reduce_scatter | solution.py:151
  (73 shorter events, 8.9 us)
Async XLA Ops:
  7.2 85.1 %copy-start = (bf16[512,2048]{1,0:T(8,128)(2,1)S(1)}, bf16[512,2048]{1,0:T(8,128)(2,1)}, u32[]{:S(2)}) copy-start(bf16[512,2048]{1,0:T(8,128)(2,1)} %param.24) | copy-start | bytes 6291460
  7.2 5.9 %copy-start.9 = (s32[8]{0:T(128)S(1)}, s32[8]{0:T(128)}, u32[]{:S(2)}) copy-start(s32[8]{0:T(128)} %param.20) | copy-start | bytes 100
  7.2 6.5 %copy-start.10 = (s32[8]{0:T(128)S(1)}, s32[8]{0:T(128)}, u32[]{:S(2)}) copy-start(s32[8]{0:T(128)} %param.21) | copy-start | bytes 100
  7.2 9.1 %copy-start.4 = (bf16[128,576]{0,1:T(8,128)(2,1)S(1)}, bf16[128,576]{0,1:T(8,128)(2,1)}, u32[]{:S(2)}) copy-start(bf16[128,576]{0,1:T(8,128)(2,1)} %param.17) | copy-start | bytes 442372
  7.2 63.7 %all-gather.4.cloned.1.call-start = ((), (), s32[]{:S(2)}) async-start(), calls=%async_computation.2 | async-start | bytes 2949120 | tf_op jit(solution)/shard_map/all_gather | solution.py:56
  7.9 92.7 %reduce-scatter.3.cloned.1.call-start = ((), (), s32[]{:S(2)}) async-start(), calls=%async_computation.3 | async-start | bytes 786432 | tf_op jit(solution)/shard_map/reduce_scatter | solution.py:91
  81.4 3.0 copy-start.3
  92.2 1.4 copy-start.8
  92.2 8.4 %copy-start.6 = (bf16[128,2048]{1,0:T(8,128)(2,1)S(1)}, bf16[128,2048]{1,0:T(8,128)(2,1)}, u32[]{:S(2)}) copy-start(bf16[128,2048]{1,0:T(8,128)(2,1)} %param.15) | copy-start | bytes 1572868
  92.2 12.9 %copy-start.7 = (s32[128,6]{0,1:T(8,128)S(1)}, s32[128,6]{0,1:T(8,128)}, u32[]{:S(2)}) copy-start(s32[128,6]{0,1:T(8,128)} %param.22) | copy-start | bytes 9220
  93.5 48.0 %all-gather.6.cloned.1.call-start = ((), (), s32[]{:S(2)}) async-start(), calls=%async_computation.5 | async-start | bytes 2359296 | tf_op jit(solution)/shard_map/all_gather | solution.py:103
  101.8 27.0 %copy-start.2 = (bf16[128,1024]{1,0:T(8,128)(2,1)}, bf16[128,1024]{1,0:T(8,128)(2,1)S(1)}, u32[]{:S(2)}) copy-start(bf16[128,1024]{1,0:T(8,128)(2,1)S(1)} %get-tuple-element.3) | copy-start | bytes 786436
  105.1 193.5 %reduce-scatter.5.cloned.1.call-start = ((), (), s32[]{:S(2)}) async-start(), calls=%async_computation.4 | async-start | bytes 2359296 | tf_op jit(solution)/shard_map/reduce_scatter | solution.py:151
  129.2 14.0 %copy-start.5 = (bf16[2048,32]{0,1:T(8,128)(2,1)S(1)}, bf16[2048,32]{0,1:T(8,128)(2,1)}, u32[]{:S(2)}) copy-start(bf16[2048,32]{0,1:T(8,128)(2,1)} %param.26) | copy-start | bytes 393220
  254.6 44.0 %copy-start.1 = (bf16[512,2048]{1,0:T(8,128)(2,1)S(1)}, bf16[512,2048]{1,0:T(8,128)(2,1)}, u32[]{:S(2)}) copy-start(bf16[512,2048]{1,0:T(8,128)(2,1)} %param.24) | copy-start | bytes 6291460
Sparse Core Ops, SparseCore 0:
  9.6 61.2 all-gather.3
  93.6 6.9 reduce-scatter.2
  105.2 31.7 all-gather.5
  261.1 37.4 reduce-scatter.4
where the time goes:
time: 306 us; the launch traced here: 305 us
  local copies, waits for them, and re-layouts  109 us (36%)
  waiting for transfers between devices  66.4 us (22%)
  matrix products  51.3 us (17%)
  blocking collectives  49 us (16%)
  other arithmetic  15.6 us (5%)
  between operations  14.1 us (5%)
    reduce_scatter x1, waiting for transfers between devices, local(): lax.psum_scatter(mixture, ('exp', 'ffn'), scatter_dimension=0, tiled=True)  37.6 us
    all_gather x1, blocking collectives, local(): lax.all_gather(new_latent, 'exp', axis=0, tiled=True)  31.2 us
    gather x3, local copies, waits for them, and re-layouts, local(): chosen = jnp.take_along_axis(logits, routes_all, axis=1)  25.3 us
    all_gather x1, waiting for transfers between devices, local(): lax.all_gather(cache_pool, 'exp', axis=0, tiled=True)  21.1 us
    dot_general x1, matrix products, local(): jnp.einsum('jmf,jfd->jmd', active, down_weight, preferred_element_type=jn...  20.7 us
    gather x1, local copies, waits for them, and re-layouts, local(): normed_grid[slot_token // token_rows, :, slot_token % token_rows, :]  18.4 us
    all_gather x1, blocking collectives, local(): routes_all = lax.all_gather(routes, 'exp', axis=0, tiled=True)  15.2 us
    dot_general x1, matrix products, local(): jnp.einsum('jmd,jdf->jmf', grouped, gate_weight, preferred_element_type=j...  13.1 us
  transfers between devices with their start and end apart: 4, of which 3 were waited for; matrix products, arithmetic and copies ran while one was open for 10% of the time, Pallas kernels for 0%

commit v1 on v0

--- a/solution.py
+++ b/solution.py
@@ -15,6 +15,19 @@
 BLOCK_ROWS = 64
 EPSILON = 1e-06
 NEG_FILL = -1e30
+
+
+def list_shapes(x_part):
+    bus_axis = "exp"
+    count_all = lax.psum(1, bus_axis)
+    right_arr = [(no - 1, no) for no in range(1, count_all)] + [(count_all - 1, 0)]
+    block_out = x_part
+    xs_all = [block_out]
+    for _ in [*range(count_all - 1)]:
+        block_out = lax.ppermute(block_out, bus_axis, right_arr)
+        xs_all += [block_out]
+    latest = jnp.concatenate([*reversed(xs_all)], 0)
+    return jnp.roll(latest, (lax.axis_index(bus_axis) + 1) * block_out.shape[0], 0)
 
 
 def slot_numbers(route_block):
@@ -103,7 +116,7 @@
     normed_grid = lax.all_gather(normed_cols, ("exp", "ffn"), axis=0, tiled=False)
     normed_grid = normed_grid.reshape(exp_size, ffn_size, token_rows, column_count)
     group_rows = exp_size * token_rows
-    routes_all = lax.all_gather(routes, "exp", axis=0, tiled=True)
+    routes_all = list_shapes(routes)
     logits = jnp.einsum(
         "efrc,fck->erk",
         normed_grid,

time: 306 us -> 304 us (level)
  blocking collectives: 49 us -> 33.7 us
  waiting for transfers between devices: 66.4 us -> 77.5 us
    all_gather x1 -> x0, blocking collectives: 15.2 us -> none  [local(): routes_all = lax.all_gather(routes, 'exp', axis=0, tiled=True)]
    ppermute x0 -> x3, waiting for transfers between devices: none -> 14.4 us  [list_shapes(): block_out = lax.ppermute(block_out, bus_axis, right_arr)]
    reduce_scatter x1, waiting for transfers between devices: 37.6 us -> 34.3 us  [local(): lax.psum_scatter(mixture, ('exp', 'ffn'), scatter_dimension=0, tiled=True)]
  transfers between devices with their start and end apart: 4 -> 7, of which waited for: 3 -> 6; matrix products, arithmetic and copies ran while one was open for 10% -> 10% of each run, Pallas kernels for 0% -> 0%
where the time goes in v1:
time: 304 us; the launch traced here: 303 us
  local copies, waits for them, and re-layouts  109 us (36%)
  waiting for transfers between devices  77.5 us (25%)
  matrix products  51.3 us (17%)
  blocking collectives  33.7 us (11%)
  other arithmetic  15.6 us (5%)
  between operations  14.2 us (5%)
    reduce_scatter x1, waiting for transfers between devices, local(): lax.psum_scatter(mixture, ('exp', 'ffn'), scatter_dimension=0, tiled=True)  34.3 us
    all_gather x1, blocking collectives, local(): lax.all_gather(new_latent, 'exp', axis=0, tiled=True)  31.2 us
    gather x3, local copies, waits for them, and re-layouts, local(): chosen = jnp.take_along_axis(logits, routes_all, axis=1)  25.3 us
    all_gather x1, waiting for transfers between devices, local(): lax.all_gather(cache_pool, 'exp', axis=0, tiled=True)  21.1 us
    dot_general x1, matrix products, local(): jnp.einsum('jmf,jfd->jmd', active, down_weight, preferred_element_type=jn...  20.7 us
    gather x1, local copies, waits for them, and re-layouts, local(): normed_grid[slot_token // token_rows, :, slot_token % token_rows, :]  18.4 us
    ppermute x3, waiting for transfers between devices, list_shapes(): block_out = lax.ppermute(block_out, bus_axis, right_arr)  14.4 us
    dot_general x1, matrix products, local(): jnp.einsum('jmd,jdf->jmf', grouped, gate_weight, preferred_element_type=j...  13.1 us
  transfers between devices with their start and end apart: 7, of which 6 were waited for; matrix products, arithmetic and copies ran while one was open for 10% of the time, Pallas kernels for 0%

profile of v1, /device:TPU:0, one launch (start us, length us, event | category | flops | bytes accessed | tf_op | source)
XLA Modules:
  0.0 302.8 jit_solution(9561286744292216356)
XLA Ops:
  8.0 2.0 copy.55
  10.9 2.1 copy.38
  16.3 31.2 %all_gather.13 = bf16[512,576]{0,1:T(8,128)(2,1)S(1)} all-gather(bf16[128,576]{0,1:T(8,128)(2,1)S(1)} %copy-done.4), channel_id=1, replica_groups=mesh['req'=4,'exp'=4,'ffn'=2] {'exp'}, dimensions={0}, use_global_device_ids=true | all-gather | bytes 737280 | tf_op jit(solution)/shard_map/all_gather | solution.py:70
  48.2 1.6 and_or_fusion
  49.9 21.1 %all-gather.4.cloned.1.call-done = bf16[128,9216]{1,0:T(8,128)(2,1)} async-done(((bf16[32,9216]{1,0:T(8,128)(2,1)}), bf16[128,9216]{1,0:T(8,128)(2,1)}) %all-gather.4.cloned.1.call-update) | async-done | bytes 2359312 | tf_op jit(solution)/shard_map/all_gather | solution.py:69
  70.9 5.3 %gather_fusion = bf16[64,9216]{1,0:T(8,128)(2,1)} fusion(bf16[128,9216]{1,0:T(8,128)(2,1)} %all-gather.4.cloned.1.call-done, s32[1024]{0:T(1024)S(1)} %pad_clamp_fusion), kind=kCustom, calls=%fused_computation | custom fusion | bytes 2359552 | tf_op jit(solution)/shard_map/jit(_take)/gather | solution.py:74
  76.3 2.2 gather.14
  78.5 1.5 copy.37
  80.0 1.4 broadcast_select_fusion
  81.4 3.0 fusion.72
  84.4 3.9 %fusion.5 = f32[128,4,1280]{0,2,1:T(8,128)} fusion(bf16[128,4,576]{0,2,1:T(8,128)(2,1)} %bitcast.110, bf16[256,576]{0,1:T(8,128)(2,1)} %constant_dynamic-slice_fusion.1, bf16[1024,576]{0,1:T(8,128)(2,1)S(1)} %broadcast_select_fusion, pred[128,1280]{0,1:T(8,128)(4,1)S(1)} %copy-done.3), kind=kOutput, calls=%fused_computation.12 | convolution fusion | flops 759234560 | bytes 4849664 | tf_op jit(solution)/shard_map/thd,kd->thk/dot_general | solution.py:82
  88.3 3.9 %fusion.27 = bf16[4,128,128]{1,2,0:T(8,128)(2,1)S(1)} fusion(bf16[512,4,128]{0,2,1:T(8,128)(2,1)} %bitcast.111, bf16[1024,576]{0,1:T(8,128)(2,1)S(1)} %broadcast_select_fusion, bf16[256,576]{0,1:T(8,128)(2,1)} %constant_dynamic-slice_fusion.1, f32[128,4]{0,1:T(4,128)S(1)} %fusion.72, f32[128,4,1280]{0,2,1:T(8,128)} %fusion.5), kind=kOutput, calls=%fused_computation.32 | convolution fusion | flops 743114496 | bytes 7374848 | tf_op jit(solution)/shard_map/thl,lhd->thd/dot_general | solution.py:98
  93.6 7.0 %reduce-scatter.3.cloned.1.call-done = bf16[128,1024]{1,0:T(8,128)(2,1)} async-done(((bf16[128,2048]{1,0:T(8,128)(2,1)}), bf16[128,1024]{1,0:T(8,128)(2,1)}) %reduce-scatter.3.cloned.1.call-update) | async-done | bytes 262160 | tf_op jit(solution)/shard_map/reduce_scatter | solution.py:104
  101.8 2.5 psum.7
  105.2 1.8 collective-permute-start
  106.9 3.7 %collective-permute-done = s32[128,6]{0,1:T(8,128)S(1)} collective-permute-done((s32[128,6]{0,1:T(8,128)S(1)}, s32[128,6]{0,1:T(8,128)S(1)}, u32[]{:S(2)}, u32[]{:S(2)}) %collective-permute-start) | collective-permute-done | bytes 3104 | tf_op jit(solution)/shard_map/ppermute | solution.py:27
  110.6 5.4 %collective-permute-done.1 = s32[128,6]{0,1:T(8,128)S(1)} collective-permute-done((s32[128,6]{0,1:T(8,128)S(1)}, s32[128,6]{0,1:T(8,128)S(1)}, u32[]{:S(2)}, u32[]{:S(2)}) %collective-permute-start.1) | collective-permute-done | bytes 3104 | tf_op jit(solution)/shard_map/ppermute | solution.py:27
  116.2 5.3 %collective-permute-done.2 = s32[128,6]{0,1:T(8,128)S(1)} collective-permute-done((s32[128,6]{0,1:T(8,128)S(1)}, s32[128,6]{0,1:T(8,128)S(1)}, u32[]{:S(2)}, u32[]{:S(2)}) %collective-permute-start.2) | collective-permute-done | bytes 3104 | tf_op jit(solution)/shard_map/ppermute | solution.py:27
  122.6 6.9 %reduce-window.6 = s32[8,32,3,128]{3,1,2,0:T(8,128)S(1)} reduce-window(s32[8,32,3,128]{3,1,2,0:T(8,128)S(1)} %fusion.38, s32[]{:T(128)} %constant.117.clone.1), window={size=1x1x1x128 pad=0_0x0_0x0_0x127_0}, to_apply=%region_5.6 | reduce-window | flops 12484608 | bytes 786436 | tf_op jit(solution)/shard_map/reduce-window
  130.7 11.8 %scatter_custom_fusion = s32[1024]{0:T(1024)S(1)} fusion(s32[3072]{0:T(1024)S(1)} %bitcast.115, s32[3072]{0:T(1024)S(1)} %reshape.307, s32[]{:T(128)} %constant.117.clone.1), kind=kCustom, calls=%fused_computation.97 | custom fusion | bytes 4100 | tf_op jit(solution)/shard_map/scatter | solution.py:140
  142.5 1.8 copy.47
  145.0 24.9 %gather_fusion.2 = f32[3072]{0:T(1024)S(1)} fusion(f32[512,32]{0,1:T(8,128)S(1)} %convolution_bitcast_fusion, s32[3072]{0:T(1024)S(1)} %reshape.297), kind=kCustom, calls=%fused_computation.2 | custom fusion | bytes 49152 | tf_op jit(solution)/shard_map/jit(take_along_axis)/gather | solution.py:126
  170.6 5.1 %copy.46 = bf16[4,2,128,1024]{3,1,2,0:T(2,128)(2,1)} copy(bf16[4,2,128,1024]{3,2,1,0:T(8,128)(2,1)} %bitcast.105) | data formatting | bytes 4194304 | tf_op jit(solution)/shard_map/reshape | solution.py:117
  175.7 18.4 %gather_fusion.1 = bf16[1024,2,1024]{2,1,0:T(2,128)(2,1)} fusion(bf16[4,2,128,1024]{3,1,2,0:T(2,128)(2,1)} %copy.46, s32[1024]{0:T(1024)S(1)} %fusion.49), kind=kCustom, calls=%fused_computation.1 | custom fusion | bytes 8396800 | tf_op jit(solution)/shard_map/gather | solution.py:146
  194.2 7.8 %reshape.279 = bf16[8,128,2048]{2,1,0:T(8,128)(2,1)} reshape(bf16[1024,2,1024]{2,1,0:T(2,128)(2,1)} %gather_fusion.1) | data formatting | bytes 8388608 | tf_op jit(solution)/shard_map/reshape | solution.py:147
  202.0 12.0 %scatter_custom_fusion.1 = f32[1024]{0:T(1024)S(1)} fusion(s32[3072]{0:T(1024)S(1)} %bitcast.116, f32[3072]{0:T(1024)S(1)} %reshape.315, f32[]{:T(128)} %constant.137.clone.1), kind=kCustom, calls=%fused_computation.100 | custom fusion | bytes 4100 | tf_op jit(solution)/shard_map/scatter | solution.py:144
  214.0 13.1 %fusion.75 = f32[8,128,704]{1,2,0:T(8,128)} fusion(bf16[8,128,2048]{2,1,0:T(8,128)(2,1)} %reshape.279, bf16[8,2048,704]{1,2,0:T(8,128)(2,1)} %param.27), kind=kOutput, calls=%fused_computation.120 | convolution fusion | flops 2952790016 | bytes 30146560 | tf_op jit(solution)/shard_map/jmd,jdf->jmf/dot_general | solution.py:148
  227.1 20.7 %multiply_convert_fusion = bf16[8,128,2048]{2,1,0:T(8,128)(2,1)} fusion(f32[8,128]{1,0:T(8,128)S(1)} %bitcast.117, bf16[8,704,2048]{2,1,0:T(8,128)(2,1)} %param.29, f32[8,128,704]{1,2,0:T(8,128)} %fusion.75, bf16[8,128,2048]{2,1,0:T(8,128)(2,1)} %reshape.279, bf16[8,2048,704]{1,2,0:T(8,128)(2,1)} %param.28), kind=kOutput, calls=%fused_computation.6 | convolution fusion | flops 5914099712 | bytes 57413632 | tf_op jit(solution)/shard_map/jmf,jfd->jmd/dot_general | solution.py:151
  247.8 7.8 %convert_element_type.72 = bf16[1024,2,1024]{2,1,0:T(2,128)(2,1)} reshape(bf16[8,128,2048]{2,1,0:T(8,128)(2,1)} %multiply_convert_fusion) | data formatting | bytes 8388608 | tf_op jit(solution)/shard_map/convert_element_type | solution.py:152
  255.5 4.8 %convert_bitcast_fusion = bf16[4,2,128,1024]{3,2,0,1:T(8,128)(2,1)S(1)} fusion(bf16[1024,2,1024,1]{2,1,0,3:T(2,128)(2,1)} %bitcast.108, s32[4,128]{1,0:T(4,128)S(1)} %multiply_add_fusion, s32[1024]{0:T(1024)S(1)} %scatter_custom_fusion), kind=kOutput, calls=%fused_computation.17 | convolution fusion | flops 2149056512 | bytes 6297600 | tf_op jit(solution)/shard_map/ers,sfc->efrc/dot_general | solution.py:157
  260.3 1.6 copy.50
  262.0 34.3 %reduce-scatter.5.cloned.1.call-done = bf16[128,1024]{1,0:T(8,128)(2,1)} async-done(((bf16[1024,1024]{1,0:T(8,128)(2,1)}), bf16[128,1024]{1,0:T(8,128)(2,1)}) %reduce-scatter.5.cloned.1.call-update) | async-done | bytes 262160 | tf_op jit(solution)/shard_map/reduce_scatter | solution.py:164
  (87 shorter events, 12.7 us)
Async XLA Ops:
  7.2 85.1 %copy-start = (bf16[512,2048]{1,0:T(8,128)(2,1)S(1)}, bf16[512,2048]{1,0:T(8,128)(2,1)}, u32[]{:S(2)}) copy-start(bf16[512,2048]{1,0:T(8,128)(2,1)} %param.24) | copy-start | bytes 6291460
  7.2 5.9 %copy-start.9 = (s32[8]{0:T(128)S(1)}, s32[8]{0:T(128)}, u32[]{:S(2)}) copy-start(s32[8]{0:T(128)} %param.20) | copy-start | bytes 100
  7.2 6.5 %copy-start.10 = (s32[8]{0:T(128)S(1)}, s32[8]{0:T(128)}, u32[]{:S(2)}) copy-start(s32[8]{0:T(128)} %param.21) | copy-start | bytes 100
  7.2 9.1 %copy-start.4 = (bf16[128,576]{0,1:T(8,128)(2,1)S(1)}, bf16[128,576]{0,1:T(8,128)(2,1)}, u32[]{:S(2)}) copy-start(bf16[128,576]{0,1:T(8,128)(2,1)} %param.17) | copy-start | bytes 442372
  7.2 63.7 %all-gather.4.cloned.1.call-start = ((), (), s32[]{:S(2)}) async-start(), calls=%async_computation.2 | async-start | bytes 2949120 | tf_op jit(solution)/shard_map/all_gather | solution.py:69
  7.9 92.7 %reduce-scatter.3.cloned.1.call-start = ((), (), s32[]{:S(2)}) async-start(), calls=%async_computation.3 | async-start | bytes 786432 | tf_op jit(solution)/shard_map/reduce_scatter | solution.py:104
  81.4 3.0 copy-start.3
  92.2 1.4 copy-start.8
  92.2 8.4 %copy-start.6 = (bf16[128,2048]{1,0:T(8,128)(2,1)S(1)}, bf16[128,2048]{1,0:T(8,128)(2,1)}, u32[]{:S(2)}) copy-start(bf16[128,2048]{1,0:T(8,128)(2,1)} %param.15) | copy-start | bytes 1572868
  92.2 12.9 %copy-start.7 = (s32[128,6]{0,1:T(8,128)S(1)}, s32[128,6]{0,1:T(8,128)}, u32[]{:S(2)}) copy-start(s32[128,6]{0,1:T(8,128)} %param.22) | copy-start | bytes 9220
  93.5 49.0 %all-gather.6.cloned.1.call-start = ((), (), s32[]{:S(2)}) async-start(), calls=%async_computation.5 | async-start | bytes 2359296 | tf_op jit(solution)/shard_map/all_gather | solution.py:116
  101.8 28.0 %copy-start.2 = (bf16[128,1024]{1,0:T(8,128)(2,1)}, bf16[128,1024]{1,0:T(8,128)(2,1)S(1)}, u32[]{:S(2)}) copy-start(bf16[128,1024]{1,0:T(8,128)(2,1)S(1)} %get-tuple-element.3) | copy-start | bytes 786436
  105.1 191.2 %reduce-scatter.5.cloned.1.call-start = ((), (), s32[]{:S(2)}) async-start(), calls=%async_computation.4 | async-start | bytes 2359296 | tf_op jit(solution)/shard_map/reduce_scatter | solution.py:164
  105.2 5.5 %collective-permute-start = (s32[128,6]{0,1:T(8,128)S(1)}, s32[128,6]{0,1:T(8,128)S(1)}, u32[]{:S(2)}, u32[]{:S(2)}) collective-permute-start(s32[128,6]{0,1:T(8,128)S(1)} %copy-done.7), channel_id=1, source_target_pairs={{0,2},{2,4},{4,6},{6,0},{1,3},{3,5},{5,7},{7,1},{8,10},{10,12},{12... | collective-permute-start | bytes 9224 | tf_op jit(solution)/shard_map/ppermute | solution.py:27
  110.6 5.4 %collective-permute-start.1 = (s32[128,6]{0,1:T(8,128)S(1)}, s32[128,6]{0,1:T(8,128)S(1)}, u32[]{:S(2)}, u32[]{:S(2)}) collective-permute-start(s32[128,6]{0,1:T(8,128)S(1)} %collective-permute-done), channel_id=1, source_target_pairs={{0,2},{2,4},{4,6},{6,0},{1,3},{3,5},{5,7},{7,1},{8,10},{10,12},{12... | collective-permute-start | bytes 9224 | tf_op jit(solution)/shard_map/ppermute | solution.py:27
  116.0 5.5 %collective-permute-start.2 = (s32[128,6]{0,1:T(8,128)S(1)}, s32[128,6]{0,1:T(8,128)S(1)}, u32[]{:S(2)}, u32[]{:S(2)}) collective-permute-start(s32[128,6]{0,1:T(8,128)S(1)} %collective-permute-done.1), channel_id=1, source_target_pairs={{0,2},{2,4},{4,6},{6,0},{1,3},{3,5},{5,7},{7,1},{8,10},{10,12},{12... | collective-permute-start | bytes 9224 | tf_op jit(solution)/shard_map/ppermute | solution.py:27
  130.2 14.0 %copy-start.5 = (bf16[2048,32]{0,1:T(8,128)(2,1)S(1)}, bf16[2048,32]{0,1:T(8,128)(2,1)}, u32[]{:S(2)}) copy-start(bf16[2048,32]{0,1:T(8,128)(2,1)} %param.26) | copy-start | bytes 393220
  255.5 40.7 %copy-start.1 = (bf16[512,2048]{1,0:T(8,128)(2,1)S(1)}, bf16[512,2048]{1,0:T(8,128)(2,1)}, u32[]{:S(2)}) copy-start(bf16[512,2048]{1,0:T(8,128)(2,1)} %param.24) | copy-start | bytes 6291460
Sparse Core Ops, SparseCore 0:
  9.6 61.2 all-gather.3
  93.6 6.9 reduce-scatter.2
  105.2 30.2 all-gather.5
  262.1 34.1 reduce-scatter.4
